TPU v7x, 512 devices: a whole 4x4x16 slice. The times are simulated.
512 devices in a mesh: dp: 4 (over z_hi, core), tm: 8 (over z_lo), height: 16 (over x, y).
Axes of the slice: x: 4, y: 4, z: 16 (z_hi: 2, z_lo: 8; z = z_hi * 8 + z_lo), core: 2. Of those that a mesh axis runs over, the one named last changes fastest.
Arguments:
- clips: bfloat16 [4, 16, 64, 128, 128], P('dp', 'tm', 'height'), may hold values from -6 to 6
- frame_counts: int32 [4, 5], P('dp'), may hold values from 1 to 9, 16 in all within a row
- conv_first: bfloat16 [3, 3, 3, 128, 128], replicated, may hold values from -0.109375 to 0.109375
- conv_down: bfloat16 [3, 3, 3, 128, 128], replicated, may hold values from -0.109375 to 0.109375
- out_cotangent: bfloat16 [4, 8, 32, 64, 128], P('dp', 'tm', 'height'), may hold values from -6 to 6
Outputs:
- encoded: bfloat16 [4, 8, 32, 64, 128], P('dp', 'tm', 'height')
- grad_first: bfloat16 [3, 3, 3, 128, 128], P(None, None, None, 'dp')
- grad_down: bfloat16 [3, 3, 3, 128, 128], P(None, None, None, 'dp')
Inputs may be any that keep to these rules, and one draw needn't show every extreme that they name: `frame_counts`: each sequence's 5 clip lengths sum to 16; in every sequence one clip has exactly 9 frames.
All inputs are finite; a program needn't handle non-finite values.
Results may differ from a plain program's by a relative error of at most 0.0059.
Values may be sent and summed in bfloat16 or wider, within the bound.
No kernel may reach another device: no remote copies, remote signals or barrier semaphores. Data moves between devices by JAX's collectives and lax.ppermute only.
A program may use at most 64 MiB of HBM per device.

v0:
```python
import math
import jax
import jax.numpy as jnp
from jax import lax
from jax.sharding import PartitionSpec as P


def padded_2(cells, sides, width):
    for axis, dim in sides:
        count = lax.axis_size(axis)
        ends = count - 1
        head = lax.slice_in_dim(cells, 0, width, axis=dim)
        tail = lax.slice_in_dim(cells, cells.shape[dim] - width, cells.shape[dim], axis=dim)
        cells = jnp.concatenate(
            [
                lax.ppermute(tail, axis, [(i, (i + 1) % count) for i in range(ends)]),
                cells,
                lax.ppermute(head, axis, [((i + 1) % count, i) for i in range(ends)]),
            ],
            axis=dim,
        )
    return cells


def shifted(value, axis, steps):
    count = lax.axis_size(axis)
    leading, last = (max(0, -steps), min(count, count - steps))
    return lax.ppermute(value, axis, [(source, source + steps) for source in range(leading, last)])


def unfold(frame_slab, stride, pad_cols):
    padded = jnp.pad(frame_slab, ((0, 0), (0, 0), pad_cols, (0, 0)))
    out_rows = (padded.shape[1] - 3) // stride + 1
    out_cols = (padded.shape[2] - 3) // stride + 1
    pieces = []
    for tap_row in range(3):
        for tap_col in range(3):
            pieces.append(
                padded[
                    :,
                    tap_row : tap_row + stride * (out_rows - 1) + 1 : stride,
                    tap_col : tap_col + stride * (out_cols - 1) + 1 : stride,
                ]
            )
    joined = jnp.concatenate(pieces, axis=-1)
    return (joined.reshape(-1, joined.shape[-1]), (frame_slab.shape[0], out_rows, out_cols))


def conv_layer(extended, weight, tap_mask, out_frames, stride, pad_cols):
    channels_out = weight.shape[-1]
    summed = None
    for tap_time in range(3):
        frame_slab = extended[tap_time : tap_time + stride * (out_frames - 1) + 1 : stride]
        columns, shape_out = unfold(frame_slab, stride, pad_cols)
        kernel = weight[tap_time].reshape(-1, channels_out)
        tap_term = jnp.dot(columns, kernel, preferred_element_type=jnp.float32).reshape(
            shape_out + (channels_out,)
        )
        tap_term = tap_term * tap_mask[:, tap_time][:, None, None, None]
        summed = tap_term if summed is None else summed + tap_term
    return summed


def weight_grad(extended, grads, tap_mask, stride, pad_cols):
    out_frames = grads.shape[0]
    blocks = []
    for tap_time in range(3):
        frame_slab = extended[tap_time : tap_time + stride * (out_frames - 1) + 1 : stride]
        columns, shape_out = unfold(frame_slab, stride, pad_cols)
        masked = grads * tap_mask[:, tap_time].astype(jnp.bfloat16)[:, None, None, None]
        blocks.append(
            jnp.dot(
                columns.T, masked.reshape(-1, grads.shape[-1]), preferred_element_type=jnp.float32
            )
        )
    stacked = jnp.stack(blocks)
    return stacked.reshape(3, 3, 3, extended.shape[-1], grads.shape[-1])


def hidden_grad(grads_ext, weight, mask_ext):
    pieces = []
    for tap_time in range(3):
        masked = grads_ext * mask_ext[:, tap_time].astype(jnp.bfloat16)[:, None, None, None]
        kernel = jnp.transpose(weight[tap_time][::-1, ::-1], (0, 1, 3, 2))
        spread = lax.conv_general_dilated(
            masked,
            kernel,
            (1, 1),
            ((2, 0), (2, 2)),
            lhs_dilation=(2, 2),
            dimension_numbers=("NHWC", "HWIO", "NHWC"),
            preferred_element_type=jnp.float32,
        )
        pieces.append(spread[:, 1:, 1:])
    even_frames = pieces[2][:-1] + pieces[0][1:]
    odd_frames = pieces[1][1:]
    merged = jnp.stack([even_frames, odd_frames], axis=1)
    return merged.reshape((2 * even_frames.shape[0],) + even_frames.shape[1:])


def positions(counts_row, frame_index):
    starts = jnp.cumsum(counts_row) - counts_row
    latest = jnp.max(jnp.where(starts[None, :] <= frame_index[:, None], starts[None, :], 0), axis=1)
    return frame_index - latest


def tap_masks(place):
    return (place[:, None] >= (2 - jnp.arange(3, dtype=jnp.int32))[None, :]).astype(jnp.float32)


def body(clips, frame_counts, conv_first, conv_down, out_cotangent):
    frames_dev = clips.shape[1]
    rows_dev = clips.shape[2]
    columns_all = clips.shape[3]
    down_frames = frames_dev // 2
    counts_row = frame_counts[0]
    first_frame = lax.axis_index("tm") * frames_dev
    frame_index = first_frame + jnp.arange(frames_dev, dtype=jnp.int32)
    first_mask = tap_masks(positions(counts_row, frame_index))
    down_index = first_frame + 2 * jnp.arange(down_frames + 1, dtype=jnp.int32)
    mask_ext = tap_masks(positions(counts_row, down_index))
    down_mask = mask_ext[:down_frames]
    with_rows = padded_2(clips[0], (("height", 1),), 1)
    earlier = shifted(with_rows, "tm", 1)
    input_ext = jnp.concatenate([earlier, with_rows], axis=0)
    pre_act = conv_layer(input_ext, conv_first, first_mask, frames_dev, 1, (1, 1))
    hidden = jax.nn.silu(pre_act).astype(jnp.bfloat16)
    above = shifted(hidden[:, rows_dev - 1 :], "height", 1)
    hidden_rows = jnp.concatenate([above, hidden], axis=1)
    hidden_past = shifted(hidden_rows, "tm", 1)
    hidden_ext = jnp.concatenate([hidden_past, hidden_rows], axis=0)
    encoded = conv_layer(hidden_ext, conv_down, down_mask, down_frames, 2, (1, 0)).astype(
        jnp.bfloat16
    )
    cells_all = (
        lax.axis_size("dp")
        * clips.shape[0]
        * down_frames
        * lax.axis_size("tm")
        * (rows_dev // 2)
        * lax.axis_size("height")
        * (columns_all // 2)
    )
    scale = 1.0 / math.sqrt(cells_all)
    grads = (out_cotangent[0].astype(jnp.float32) * scale).astype(jnp.bfloat16)
    down_local = weight_grad(hidden_ext, grads, down_mask, 2, (1, 0))
    below = shifted(grads[:, 0:1], "height", -1)
    grads_rows = jnp.concatenate([grads, below], axis=1)
    grads_next = shifted(grads_rows, "tm", -1)
    grads_ext = jnp.concatenate([grads_rows, grads_next], axis=0)
    back_hidden = hidden_grad(grads_ext, conv_down, mask_ext).astype(jnp.bfloat16)
    sigma = jax.nn.sigmoid(pre_act)
    pre_grad = (back_hidden.astype(jnp.float32) * sigma * (1.0 + pre_act * (1.0 - sigma))).astype(
        jnp.bfloat16
    )
    first_local = weight_grad(input_ext, pre_grad, first_mask, 1, (1, 1))
    share = conv_first.shape[3] // lax.axis_size("dp")
    quarters = lax.axis_size("dp")

    def by_quarter(term):
        term = term.reshape(27, quarters, share, term.shape[-1])
        return jnp.transpose(term, (1, 0, 2, 3)).reshape(quarters, -1)

    stacked = jnp.concatenate([by_quarter(first_local), by_quarter(down_local)], axis=1)
    rows_n, frames_n = (lax.axis_size("height"), lax.axis_size("tm"))
    piece = stacked.reshape(quarters, rows_n, frames_n, -1)
    piece = lax.psum_scatter(piece, "height", scatter_dimension=1, tiled=True)
    piece = lax.psum_scatter(piece, "tm", scatter_dimension=2, tiled=True)
    piece = lax.psum_scatter(piece, "dp", scatter_dimension=0, tiled=True)
    piece = piece.astype(jnp.bfloat16)
    piece = lax.all_gather(piece, "tm", axis=2, tiled=True)
    gathered = lax.all_gather(piece, "height", axis=1, tiled=True).reshape(-1)
    half = gathered.shape[0] // 2
    kernel_shape = (3, 3, 3, share, conv_first.shape[-1])
    summed_first = gathered[:half].reshape(kernel_shape)
    summed_down = gathered[half:].reshape(kernel_shape)
    return (encoded[None], summed_first, summed_down)


def solution(mesh):
    in_specs = (
        P("dp", "tm", "height", None, None),
        P("dp", None),
        P(),
        P(),
        P("dp", "tm", "height", None, None),
    )
    out_specs = (
        P("dp", "tm", "height", None, None),
        P(None, None, None, "dp", None),
        P(None, None, None, "dp", None),
    )
    return jax.shard_map(body, mesh=mesh, in_specs=in_specs, out_specs=out_specs, check_vma=False)
```

profile of v0, /device:TPU:32, one launch (start us, length us, event | category | flops | bytes accessed | tf_op | source)
XLA Modules:
  0.0 460.8 jit_solution(5492218654866860973)
XLA Ops:
  8.1 3.5 collective-permute-start
  11.6 1.3 collective-permute-start.1
  13.7 1.3 collective-permute-start.5
  21.7 5.2 %collective-permute-start.6 = (bf16[1,3,64,128]{3,2,1,0:T(8,128)(2,1)S(1)}, bf16[1,3,64,128]{3,2,1,0:T(8,128)(2,1)S(1)}, u32[]{:S(2)}, u32[]{:S(2)}) collective-permute-start(bf16[1,3,64,128]{3,2,1,0:T(8,128)(2,1)S(1)} %pad_maximum_fusion.8), channel_id=1, source_target_pairs={{16,0},{32,16},{48,32},{64,48},{80,64},{96,80},{112,96},{17,1},{33... | collective-permute-start | bytes 147464 | tf_op jit(solution)/shard_map/ppermute | solution.py:28
  27.0 2.1 collective-permute-start.2
  29.2 1.3 multiply_bitcast_fusion.1
  33.1 3.8 collective-permute-done.2
  43.9 5.2 %collective-permute-start.3 = (bf16[2,1,128,128]{3,2,1,0:T(8,128)(2,1)S(1)}, bf16[2,1,128,128]{3,2,1,0:T(8,128)(2,1)S(1)}, u32[]{:S(2)}, u32[]{:S(2)}) collective-permute-start(bf16[2,1,128,128]{3,2,1,0:T(8,128)(2,1)S(1)} %slice.447), channel_id=1, source_target_pairs={{0,1},{1,2},{2,3},{3,4},{4,5},{5,6},{6,7},{7,8},{8,9},{9,10},{10,1... | collective-permute-start | bytes 196616 | tf_op jit(solution)/shard_map/ppermute | solution.py:28
  49.2 1.4 copy.96
  50.6 1.9 concatenate.66
  53.9 3.2 collective-permute-start.4
  57.5 5.3 %collective-permute-done.4 = bf16[2,5,128,128]{3,2,1,0:T(8,128)(2,1)S(1)} collective-permute-done((bf16[2,5,128,128]{3,2,1,0:T(8,128)(2,1)S(1)}, bf16[2,5,128,128]{3,2,1,0:T(8,128)(2,1)S(1)}, u32[]{:S(2)}, u32[]{:S(2)}) %collective-permute-start.4) | collective-permute-done | bytes 327712 | tf_op jit(solution)/shard_map/ppermute | solution.py:28
  80.7 1.4 copy.95
  82.1 2.9 concatenate.67
  85.0 3.6 pad_maximum_fusion
  88.7 1.3 dynamic-slice
  93.5 132.0 %all-reduce.12.cloned.1.call-done = f32[4,16,8,1728]{3,2,1,0:T(8,128)} async-done(((f32[4,16,8,1728]{3,2,1,0:T(8,128)}), f32[4,16,8,1728]{3,2,1,0:T(8,128)}) %all-reduce.12.cloned.1.call-update) | async-done | bytes 3538960
  225.5 1.6 constant_dynamic-slice_fusion.1
  228.8 1.4 fusion.8
  230.2 112.4 %all-reduce.14.cloned.1.call-done = f32[4,1,8,1728]{3,0,1,2:T(4,128)} async-done(((f32[4,1,8,1728]{3,0,1,2:T(4,128)}), f32[4,1,8,1728]{3,0,1,2:T(4,128)}) %all-reduce.14.cloned.1.call-update) | async-done | bytes 221200
  342.6 1.4 constant_dynamic-slice_fusion
  344.0 35.2 %all-reduce.8 = bf16[4,1,1,1728]{3,2,1,0:T(2,128)(2,1)S(1)} all-reduce(f32[4,1,1,1728]{3,2,1,0:T(1,128)S(1)} %copy.72), channel_id=4, replica_groups=mesh['dp'=4,'tm'=8,'height'=16] {'dp'}, use_global_device_ids=true, to_apply=%region_5.6.clone | all-reduce | flops 6912 | bytes 41472
  379.9 48.0 %all_gather.6 = bf16[1,1,8,1728]{3,1,0,2:T(2,128)(2,1)S(1)} all-gather(bf16[1,1,1,1728]{3,1,0,2:T(2,128)(2,1)S(1)} %fusion.64), channel_id=1, replica_groups=mesh['dp'=4,'tm'=8,'height'=16] {'tm'}, dimensions={2}, use_global_device_ids=true | all-gather | bytes 31104 | tf_op jit(solution)/shard_map/all_gather | solution.py:171
  427.9 24.0 %all_gather.7 = bf16[1,16,8,1728]{3,2,0,1:T(8,128)(2,1)S(1)} all-gather(bf16[1,1,8,1728]{3,2,0,1:T(8,128)(2,1)S(1)} %copy.74), channel_id=1, replica_groups=mesh['dp'=4,'tm'=8,'height'=16] {'height'}, dimensions={1}, use_global_device_ids=true | all-gather | bytes 470016 | tf_op jit(solution)/shard_map/all_gather | solution.py:172
  (174 shorter events, 43.3 us)
Async XLA Ops:
  7.2 19.8 %copy-start = (bf16[1,2,4,128,128]{4,3,2,1,0:T(8,128)(2,1)S(1)}, bf16[1,2,4,128,128]{4,3,2,1,0:T(8,128)(2,1)}, u32[]{:S(2)}) copy-start(bf16[1,2,4,128,128]{4,3,2,1,0:T(8,128)(2,1)} %param.5) | copy-start | bytes 786436
  7.2 218.3 %all-reduce.12.cloned.1.call-start = ((), (), s32[]{:S(2)}) async-start(), calls=%async_computation | async-start | bytes 7340032
  8.1 18.8 %collective-permute-start = (bf16[2,1,128,128]{3,2,1,0:T(8,128)(2,1)S(1)}, bf16[2,1,128,128]{3,2,1,0:T(8,128)(2,1)S(1)}, u32[]{:S(2)}, u32[]{:S(2)}) collective-permute-start(bf16[2,1,128,128]{3,2,1,0:T(8,128)(2,1)S(1)} %get-tuple-element.17), channel_id=1, source_target_pairs={{0,1},{1,2},{2,3},{3,4},{4,5},{5,6},{6,7},{7,8},{8,9},{9,10},{10,1... | collective-permute-start | bytes 196616 | tf_op jit(solution)/shard_map/ppermute | solution.py:16
  11.6 15.3 %collective-permute-start.1 = (bf16[2,1,128,128]{3,2,1,0:T(8,128)(2,1)S(1)}, bf16[2,1,128,128]{3,2,1,0:T(8,128)(2,1)S(1)}, u32[]{:S(2)}, u32[]{:S(2)}) collective-permute-start(bf16[2,1,128,128]{3,2,1,0:T(8,128)(2,1)S(1)} %get-tuple-element.18), channel_id=1, source_target_pairs={{1,0},{2,1},{3,2},{4,3},{5,4},{6,5},{7,6},{8,7},{9,8},{10,9},{11,1... | collective-permute-start | bytes 196616 | tf_op jit(solution)/shard_map/ppermute | solution.py:18
  13.7 8.0 %collective-permute-start.5 = (bf16[1,1,64,128]{3,2,1,0:T(8,128)(2,1)S(1)}, bf16[1,1,64,128]{3,2,1,0:T(8,128)(2,1)S(1)}, u32[]{:S(2)}, u32[]{:S(2)}) collective-permute-start(bf16[1,1,64,128]{3,2,1,0:T(8,128)(2,1)S(1)} %slice.452), channel_id=1, source_target_pairs={{1,0},{2,1},{3,2},{4,3},{5,4},{6,5},{7,6},{8,7},{9,8},{10,9},{11,1... | collective-permute-start | bytes 49160 | tf_op jit(solution)/shard_map/ppermute | solution.py:28
  21.7 7.5 %collective-permute-start.6 = (bf16[1,3,64,128]{3,2,1,0:T(8,128)(2,1)S(1)}, bf16[1,3,64,128]{3,2,1,0:T(8,128)(2,1)S(1)}, u32[]{:S(2)}, u32[]{:S(2)}) collective-permute-start(bf16[1,3,64,128]{3,2,1,0:T(8,128)(2,1)S(1)} %pad_maximum_fusion.8), channel_id=1, source_target_pairs={{16,0},{32,16},{48,32},{64,48},{80,64},{96,80},{112,96},{17,1},{33... | collective-permute-start | bytes 147464 | tf_op jit(solution)/shard_map/ppermute | solution.py:28
  27.0 4.3 copy-start.1
  27.0 4.3 copy-start.4
  27.0 9.8 %collective-permute-start.2 = (bf16[2,6,128,128]{3,2,1,0:T(8,128)(2,1)S(1)}, bf16[2,6,128,128]{3,2,1,0:T(8,128)(2,1)S(1)}, u32[]{:S(2)}, u32[]{:S(2)}) collective-permute-start(bf16[2,6,128,128]{3,2,1,0:T(8,128)(2,1)S(1)} %pad_maximum_fusion.4), channel_id=1, source_target_pairs={{0,16},{16,32},{32,48},{48,64},{64,80},{80,96},{96,112},{1,17},{17... | collective-permute-start | bytes 1179656 | tf_op jit(solution)/shard_map/ppermute | solution.py:28
  43.9 8.6 %collective-permute-start.3 = (bf16[2,1,128,128]{3,2,1,0:T(8,128)(2,1)S(1)}, bf16[2,1,128,128]{3,2,1,0:T(8,128)(2,1)S(1)}, u32[]{:S(2)}, u32[]{:S(2)}) collective-permute-start(bf16[2,1,128,128]{3,2,1,0:T(8,128)(2,1)S(1)} %slice.447), channel_id=1, source_target_pairs={{0,1},{1,2},{2,3},{3,4},{4,5},{5,6},{6,7},{7,8},{8,9},{9,10},{10,1... | collective-permute-start | bytes 196616 | tf_op jit(solution)/shard_map/ppermute | solution.py:28
  50.6 6.6 %copy-start.3 = (bf16[1,1,2,64,128]{4,3,2,1,0:T(8,128)(2,1)S(1)}, bf16[1,1,2,64,128]{4,3,2,1,0:T(8,128)(2,1)}, u32[]{:S(2)}) copy-start(bf16[1,1,2,64,128]{4,3,2,1,0:T(8,128)(2,1)} %param.9) | copy-start | bytes 98308
  53.9 9.0 %collective-permute-start.4 = (bf16[2,5,128,128]{3,2,1,0:T(8,128)(2,1)S(1)}, bf16[2,5,128,128]{3,2,1,0:T(8,128)(2,1)S(1)}, u32[]{:S(2)}, u32[]{:S(2)}) collective-permute-start(bf16[2,5,128,128]{3,2,1,0:T(8,128)(2,1)S(1)} %pad_maximum_fusion.3), channel_id=1, source_target_pairs={{0,16},{16,32},{32,48},{48,64},{64,80},{80,96},{96,112},{1,17},{17... | collective-permute-start | bytes 983048 | tf_op jit(solution)/shard_map/ppermute | solution.py:28
  88.6 3.9 copy-start.2
  88.7 253.9 %all-reduce.14.cloned.1.call-start = ((), (), s32[]{:S(2)}) async-start(), calls=%async_computation.1 | async-start | bytes 458752
Sparse Core Ops, SparseCore 0:
  88.8 136.6 all-reduce.11
  228.4 114.1 all-reduce.13
where the time goes:
time: 462 us; the launch traced here: 461 us
  waiting for transfers between devices  253 us (55%)
  blocking collectives  107 us (23%)
  local copies, waits for them, and re-layouts  43.2 us (9%)
  starting transfers between devices  21.8 us (5%)
  between operations  16.9 us (4%)
  matrix products  10 us (2%)
  other arithmetic  8.16 us (2%)
    unnamed x4, waiting for transfers between devices  244 us
    all_gather x1, blocking collectives, body(): piece = lax.all_gather(piece, 'tm', axis=2, tiled=True)  48 us
    unnamed x1, blocking collectives  35.2 us
    all_gather x1, blocking collectives, body(): gathered = lax.all_gather(piece, 'height', axis=1, tiled=True).reshape(-1)  24 us
    unnamed x66, local copies, waits for them, and re-layouts  17 us
    ppermute x5, starting transfers between devices, shifted(): lax.ppermute(value, axis, [(source, source + steps) for source in range(l...  17 us
    slice x27, local copies, waits for them, and re-layouts, unfold(): padded[:, tap_row:tap_row + stride * (out_rows - 1) + 1:stride, tap_col:t...  9.5 us
  transfers between devices with their start and end apart: 9, of which 4 were waited for; matrix products, arithmetic and copies ran while one was open for 4% of the time, Pallas kernels for 0%

commit v1 on v0

--- a/solution.py
+++ b/solution.py
@@ -168,7 +168,10 @@
     piece = lax.psum_scatter(piece, "tm", scatter_dimension=2, tiled=True)
     piece = lax.psum_scatter(piece, "dp", scatter_dimension=0, tiled=True)
     piece = piece.astype(jnp.bfloat16)
-    piece = lax.all_gather(piece, "tm", axis=2, tiled=True)
+    devices = lax.axis_size("tm")
+    shards = jnp.stack([piece for _ in range(devices)])
+    shards = lax.all_to_all(shards, "tm", split_axis=0, concat_axis=0)
+    piece = jnp.concatenate(shards, axis=2)
     gathered = lax.all_gather(piece, "height", axis=1, tiled=True).reshape(-1)
     half = gathered.shape[0] // 2
     kernel_shape = (3, 3, 3, share, conv_first.shape[-1])

time: 462 us -> 438 us (0.948)
  the two profiles are of different devices: /device:TPU:32 before, /device:TPU:2 now
where the time goes in v1:
time: 438 us; the launch traced here: 437 us
  waiting for transfers between devices  266 us (61%)
  blocking collectives  55.9 us (13%)
  local copies, waits for them, and re-layouts  44.6 us (10%)
  starting transfers between devices  34.8 us (8%)
  between operations  16.9 us (4%)
  matrix products  10 us (2%)
  other arithmetic  8.96 us (2%)
    unnamed x4, waiting for transfers between devices  247 us
    unnamed x1, blocking collectives  32.2 us
    all_gather x1, blocking collectives, body(): gathered = lax.all_gather(piece, 'height', axis=1, tiled=True).reshape(-1)  23.7 us
    unnamed x68, local copies, waits for them, and re-layouts  17.8 us
    ppermute x5, starting transfers between devices, shifted(): lax.ppermute(value, axis, [(source, source + steps) for source in range(l...  16.4 us
    all_to_all x1, starting transfers between devices, body(): shards = lax.all_to_all(shards, 'tm', split_axis=0, concat_axis=0)  10.3 us
    slice x27, local copies, waits for them, and re-layouts, unfold(): padded[:, tap_row:tap_row + stride * (out_rows - 1) + 1:stride, tap_col:t...  9.51 us
    ppermute x5, waiting for transfers between devices, shifted(): lax.ppermute(value, axis, [(source, source + steps) for source in range(l...  9.2 us
  transfers between devices with their start and end apart: 10, of which 6 were waited for; matrix products, arithmetic and copies ran while one was open for 5% of the time, Pallas kernels for 0%

profile of v1, /device:TPU:2, one launch (start us, length us, event | category | flops | bytes accessed | tf_op | source)
XLA Modules:
  0.0 436.6 jit_solution(6358233052005914635)
XLA Ops:
  8.1 3.5 collective-permute-start
  11.6 4.5 %collective-permute-start.1 = (bf16[2,1,128,128]{3,2,1,0:T(8,128)(2,1)S(1)}, bf16[2,1,128,128]{3,2,1,0:T(8,128)(2,1)S(1)}, u32[]{:S(2)}, u32[]{:S(2)}) collective-permute-start(bf16[2,1,128,128]{3,2,1,0:T(8,128)(2,1)S(1)} %get-tuple-element.18), channel_id=1, source_target_pairs={{1,0},{2,1},{3,2},{4,3},{5,4},{6,5},{7,6},{8,7},{9,8},{10,9},{11,1... | collective-permute-start | bytes 196616 | tf_op jit(solution)/shard_map/ppermute | solution.py:18
  16.9 2.8 collective-permute-start.5
  27.8 4.7 %collective-permute-start.2 = (bf16[2,6,128,128]{3,2,1,0:T(8,128)(2,1)S(1)}, bf16[2,6,128,128]{3,2,1,0:T(8,128)(2,1)S(1)}, u32[]{:S(2)}, u32[]{:S(2)}) collective-permute-start(bf16[2,6,128,128]{3,2,1,0:T(8,128)(2,1)S(1)} %pad_maximum_fusion.4), channel_id=1, source_target_pairs={{0,16},{16,32},{32,48},{48,64},{64,80},{80,96},{96,112},{1,17},{17... | collective-permute-start | bytes 1179656 | tf_op jit(solution)/shard_map/ppermute | solution.py:28
  36.5 3.4 collective-permute-done.2
  47.0 3.1 collective-permute-start.3
  50.2 1.4 copy.114
  51.6 1.9 concatenate.66
  53.4 1.8 collective-permute-done.3
  56.6 4.6 %collective-permute-start.4 = (bf16[2,5,128,128]{3,2,1,0:T(8,128)(2,1)S(1)}, bf16[2,5,128,128]{3,2,1,0:T(8,128)(2,1)S(1)}, u32[]{:S(2)}, u32[]{:S(2)}) collective-permute-start(bf16[2,5,128,128]{3,2,1,0:T(8,128)(2,1)S(1)} %pad_maximum_fusion.3), channel_id=1, source_target_pairs={{0,16},{16,32},{32,48},{48,64},{64,80},{80,96},{96,112},{1,17},{17... | collective-permute-start | bytes 983048 | tf_op jit(solution)/shard_map/ppermute | solution.py:28
  61.6 3.9 collective-permute-done.4
  83.4 1.4 copy.113
  84.8 2.9 concatenate.67
  87.7 3.6 pad_maximum_fusion
  91.4 1.3 dynamic-slice
  96.3 129.1 %all-reduce.12.cloned.1.call-done = f32[4,16,8,1728]{3,2,1,0:T(8,128)} async-done(((f32[4,16,8,1728]{3,2,1,0:T(8,128)}), f32[4,16,8,1728]{3,2,1,0:T(8,128)}) %all-reduce.12.cloned.1.call-update) | async-done | bytes 3538960
  225.4 1.6 constant_dynamic-slice_fusion.1
  228.6 118.1 %all-reduce.14.cloned.1.call-done = f32[4,1,8,1728]{3,0,1,2:T(4,128)} async-done(((f32[4,1,8,1728]{3,0,1,2:T(4,128)}), f32[4,1,8,1728]{3,0,1,2:T(4,128)}) %all-reduce.14.cloned.1.call-update) | async-done | bytes 221200
  346.6 1.4 constant_dynamic-slice_fusion
  348.1 32.2 %all-reduce.8 = bf16[4,1,1,1728]{3,2,1,0:T(2,128)(2,1)S(1)} all-reduce(f32[4,1,1,1728]{3,2,1,0:T(1,128)S(1)} %copy.91), channel_id=5, replica_groups=mesh['dp'=4,'tm'=8,'height'=16] {'dp'}, use_global_device_ids=true, to_apply=%region_5.6.clone | all-reduce | flops 6912 | bytes 41472
  383.1 10.3 %all-to-all-start = ((bf16[8,2,864]{2,1,0:T(2,128)(2,1)}), bf16[8,2,864]{2,1,0:T(2,128)(2,1)S(1)}, u32[]{:S(2)}, u32[]{:S(2)}) async-start(bf16[8,2,864]{2,1,0:T(2,128)(2,1)} %reshape.274), calls=%async_computation | async-start | bytes 57344 | tf_op jit(solution)/shard_map/all_to_all | solution.py:173
  393.4 1.5 fusion.8
  394.8 9.1 %all-to-all-done = bf16[8,2,864]{2,1,0:T(2,128)(2,1)S(1)} async-done(((bf16[8,2,864]{2,1,0:T(2,128)(2,1)}), bf16[8,2,864]{2,1,0:T(2,128)(2,1)S(1)}, u32[]{:S(2)}, u32[]{:S(2)}) %all-to-all-start) | async-done | bytes 27680 | tf_op jit(solution)/shard_map/all_to_all | solution.py:173
  404.1 23.7 %all-gather = bf16[128,1,1,1,1728]{4,0,3,2,1:T(8,128)(2,1)S(1)} all-gather(bf16[8,1,1,1,1728]{4,0,3,2,1:T(8,128)(2,1)S(1)} %copy.92), channel_id=2, replica_groups=mesh['dp'=4,'tm'=8,'height'=16] {'height'}, dimensions={0}, use_global_device_ids=true | all-gather | bytes 470016 | tf_op jit(solution)/shard_map/all_gather | solution.py:175
  (180 shorter events, 48.0 us)
Async XLA Ops:
  7.2 20.5 %copy-start = (bf16[1,2,4,128,128]{4,3,2,1,0:T(8,128)(2,1)S(1)}, bf16[1,2,4,128,128]{4,3,2,1,0:T(8,128)(2,1)}, u32[]{:S(2)}) copy-start(bf16[1,2,4,128,128]{4,3,2,1,0:T(8,128)(2,1)} %param.5) | copy-start | bytes 786436
  7.2 218.2 %all-reduce.12.cloned.1.call-start = ((), (), s32[]{:S(2)}) async-start(), calls=%async_computation.1 | async-start | bytes 7340032
  8.1 19.5 %collective-permute-start = (bf16[2,1,128,128]{3,2,1,0:T(8,128)(2,1)S(1)}, bf16[2,1,128,128]{3,2,1,0:T(8,128)(2,1)S(1)}, u32[]{:S(2)}, u32[]{:S(2)}) collective-permute-start(bf16[2,1,128,128]{3,2,1,0:T(8,128)(2,1)S(1)} %get-tuple-element.17), channel_id=1, source_target_pairs={{0,1},{1,2},{2,3},{3,4},{4,5},{5,6},{6,7},{7,8},{8,9},{9,10},{10,1... | collective-permute-start | bytes 196616 | tf_op jit(solution)/shard_map/ppermute | solution.py:16
  11.6 16.1 %collective-permute-start.1 = (bf16[2,1,128,128]{3,2,1,0:T(8,128)(2,1)S(1)}, bf16[2,1,128,128]{3,2,1,0:T(8,128)(2,1)S(1)}, u32[]{:S(2)}, u32[]{:S(2)}) collective-permute-start(bf16[2,1,128,128]{3,2,1,0:T(8,128)(2,1)S(1)} %get-tuple-element.18), channel_id=1, source_target_pairs={{1,0},{2,1},{3,2},{4,3},{5,4},{6,5},{7,6},{8,7},{9,8},{10,9},{11,1... | collective-permute-start | bytes 196616 | tf_op jit(solution)/shard_map/ppermute | solution.py:18
  16.9 9.5 %collective-permute-start.5 = (bf16[1,1,64,128]{3,2,1,0:T(8,128)(2,1)S(1)}, bf16[1,1,64,128]{3,2,1,0:T(8,128)(2,1)S(1)}, u32[]{:S(2)}, u32[]{:S(2)}) collective-permute-start(bf16[1,1,64,128]{3,2,1,0:T(8,128)(2,1)S(1)} %slice.452), channel_id=1, source_target_pairs={{1,0},{2,1},{3,2},{4,3},{5,4},{6,5},{7,6},{8,7},{9,8},{10,9},{11,1... | collective-permute-start | bytes 49160 | tf_op jit(solution)/shard_map/ppermute | solution.py:28
  26.4 6.2 %collective-permute-start.6 = (bf16[1,3,64,128]{3,2,1,0:T(8,128)(2,1)S(1)}, bf16[1,3,64,128]{3,2,1,0:T(8,128)(2,1)S(1)}, u32[]{:S(2)}, u32[]{:S(2)}) collective-permute-start(bf16[1,3,64,128]{3,2,1,0:T(8,128)(2,1)S(1)} %pad_maximum_fusion.8), channel_id=1, source_target_pairs={{16,0},{32,16},{48,32},{64,48},{80,64},{96,80},{112,96},{17,1},{33... | collective-permute-start | bytes 147464 | tf_op jit(solution)/shard_map/ppermute | solution.py:28
  27.8 6.9 %copy-start.1 = (bf16[3,3,3,128,128]{4,3,2,1,0:T(8,128)(2,1)S(1)}, bf16[3,3,3,128,128]{4,3,2,1,0:T(8,128)(2,1)}, u32[]{:S(2)}) copy-start(bf16[3,3,3,128,128]{4,3,2,1,0:T(8,128)(2,1)} %param.8) | copy-start | bytes 2654212
  27.8 6.9 %copy-start.4 = (pred[8,18]{0,1:T(8,128)(4,1)S(1)}, pred[8,18]{0,1:T(8,128)(4,1)}, u32[]{:S(2)}) copy-start(pred[8,18]{0,1:T(8,128)(4,1)} %constant.53) | copy-start | bytes 436
  27.8 12.1 %collective-permute-start.2 = (bf16[2,6,128,128]{3,2,1,0:T(8,128)(2,1)S(1)}, bf16[2,6,128,128]{3,2,1,0:T(8,128)(2,1)S(1)}, u32[]{:S(2)}, u32[]{:S(2)}) collective-permute-start(bf16[2,6,128,128]{3,2,1,0:T(8,128)(2,1)S(1)} %pad_maximum_fusion.4), channel_id=1, source_target_pairs={{0,16},{16,32},{32,48},{48,64},{64,80},{80,96},{96,112},{1,17},{17... | collective-permute-start | bytes 1179656 | tf_op jit(solution)/shard_map/ppermute | solution.py:28
  47.0 8.3 %collective-permute-start.3 = (bf16[2,1,128,128]{3,2,1,0:T(8,128)(2,1)S(1)}, bf16[2,1,128,128]{3,2,1,0:T(8,128)(2,1)S(1)}, u32[]{:S(2)}, u32[]{:S(2)}) collective-permute-start(bf16[2,1,128,128]{3,2,1,0:T(8,128)(2,1)S(1)} %slice.447), channel_id=1, source_target_pairs={{0,1},{1,2},{2,3},{3,4},{4,5},{5,6},{6,7},{7,8},{8,9},{9,10},{10,1... | collective-permute-start | bytes 196616 | tf_op jit(solution)/shard_map/ppermute | solution.py:28
  51.5 9.8 %copy-start.3 = (bf16[1,1,2,64,128]{4,3,2,1,0:T(8,128)(2,1)S(1)}, bf16[1,1,2,64,128]{4,3,2,1,0:T(8,128)(2,1)}, u32[]{:S(2)}) copy-start(bf16[1,1,2,64,128]{4,3,2,1,0:T(8,128)(2,1)} %param.9) | copy-start | bytes 98308
  56.6 9.0 %collective-permute-start.4 = (bf16[2,5,128,128]{3,2,1,0:T(8,128)(2,1)S(1)}, bf16[2,5,128,128]{3,2,1,0:T(8,128)(2,1)S(1)}, u32[]{:S(2)}, u32[]{:S(2)}) collective-permute-start(bf16[2,5,128,128]{3,2,1,0:T(8,128)(2,1)S(1)} %pad_maximum_fusion.3), channel_id=1, source_target_pairs={{0,16},{16,32},{32,48},{48,64},{64,80},{80,96},{96,112},{1,17},{17... | collective-permute-start | bytes 983048 | tf_op jit(solution)/shard_map/ppermute | solution.py:28
  91.3 3.9 copy-start.2
  91.4 255.3 %all-reduce.14.cloned.1.call-start = ((), (), s32[]{:S(2)}) async-start(), calls=%async_computation.2 | async-start | bytes 458752
  383.1 20.9 %all-to-all-start = ((bf16[8,2,864]{2,1,0:T(2,128)(2,1)}), bf16[8,2,864]{2,1,0:T(2,128)(2,1)S(1)}, u32[]{:S(2)}, u32[]{:S(2)}) async-start(bf16[8,2,864]{2,1,0:T(2,128)(2,1)} %reshape.274), calls=%async_computation | async-start | bytes 57344 | tf_op jit(solution)/shard_map/all_to_all | solution.py:173
Sparse Core Ops, SparseCore 0:
  91.5 133.8 all-reduce.11
  228.3 118.2 all-reduce.13
